TPU v7x, 256 devices: a whole 4x4x8 slice. The times are simulated.
256 devices in a mesh: dp: 4 (over y), head: 4 (over x), seq: 16 (over z, core).
Axes of the slice: x: 4, y: 4, z: 8, core: 2. Of those that a mesh axis runs over, the one named last changes fastest.
Arguments:
- q_dense: bfloat16 [32768, 8, 128], P(('dp', 'seq'), 'head'), parts along dimension 0, may hold values from -108 to 108
- k_dense: bfloat16 [32768, 8, 128], P(('dp', 'seq'), 'head'), parts along dimension 0, may hold values from -4 to 4
- v_dense: bfloat16 [32768, 8, 128], P(('dp', 'seq'), 'head'), parts along dimension 0, may hold values from -4 to 4
- q_expert: bfloat16 [32768, 12, 128], P(('dp', 'seq'), 'head'), parts along dimension 0, may hold values from -108 to 108
- k_expert: bfloat16 [32768, 12, 128], P(('dp', 'seq'), 'head'), parts along dimension 0, may hold values from -4 to 4
- v_expert: bfloat16 [32768, 12, 128], P(('dp', 'seq'), 'head'), parts along dimension 0, may hold values from -4 to 4
- gate_logit: bfloat16 [12, 32768], P('head', ('dp', 'seq')), parts along dimension 1, may hold values from -8 to 8
- selection: int32 [12, 2048], P('head', 'dp'), parts along dimension 1, may hold values from 0 to 8191, as said below
Outputs:
- dense_out: bfloat16 [32768, 8, 128], P(('dp', 'seq'), 'head'), parts along dimension 0
- expert_out: bfloat16 [32768, 12, 128], P(('dp', 'seq'), 'head'), parts along dimension 0
There are 4 independent parts, one for each index of `dp`. A program takes and returns all parts, laid end to end along the dimension named above; each array names one. Nothing has to cross between parts.
Inputs may be any that keep to these rules, and one draw needn't show every extreme that they name: `selection`: each row lists 512 distinct token positions in increasing order; every row holds the first and the last token.
All inputs are finite; a program needn't handle non-finite values.
Results may differ from a plain program's by a relative error of at most 0.0055.
Values may be sent and summed in bfloat16 or wider, within the bound.
No kernel may reach another device: no remote copies, remote signals or barrier semaphores. Data moves between devices by JAX's collectives and lax.ppermute only.
A program may use at most 64 MiB of HBM per device.

v0:
```python
import math
import jax
import jax.numpy as jnp
from jax import lax
from jax.sharding import PartitionSpec as P

NEGATIVE = -1e30


def plain_rows(rows, tok_rows, count):
    return rows


def online_update(state, queries, query_pos, keys, values, key_pos, scale):
    leading, total, summed = state
    scores = jnp.einsum("qhd,khd->qhk", queries, keys, preferred_element_type=jnp.float32) * scale
    visible = key_pos[None, None, :] <= query_pos[:, None, None]
    scores = jnp.where(visible, scores, NEGATIVE)
    new_leading = jnp.maximum(leading, jnp.max(scores, axis=2))
    shrink = jnp.exp(leading - new_leading)
    weights = jnp.where(visible, jnp.exp(scores - new_leading[:, :, None]), 0.0)
    total = total * shrink + jnp.sum(weights, axis=2)
    moved = jnp.einsum(
        "qhk,khd->qhd", weights.astype(jnp.bfloat16), values, preferred_element_type=jnp.float32
    )
    return (new_leading, total, summed * shrink[:, :, None] + moved)


def dense_heads(queries, keys, values, position_map):
    tok_rows, heads, width = queries.shape
    count = lax.axis_size("seq")
    half_rows = tok_rows // 2
    own_rows = lax.axis_index("seq") * tok_rows + jnp.arange(tok_rows, dtype=jnp.int32)
    query_pos = position_map(own_rows, tok_rows, count).reshape(2, half_rows)
    groups = queries.reshape(2, half_rows, heads, width)
    scale = 1.0 / math.sqrt(width)
    blank = (
        jnp.full((half_rows, heads), NEGATIVE, jnp.float32),
        jnp.zeros((half_rows, heads), jnp.float32),
        jnp.zeros((half_rows, heads, width), jnp.float32),
    )
    key_rows = lax.all_gather(keys, "seq", axis=0, tiled=True)
    value_rows = lax.all_gather(values, "seq", axis=0, tiled=True)
    length = key_rows.shape[0]
    block = math.gcd(length, 512)
    count_blocks = length // block
    key_pos = position_map(jnp.arange(length, dtype=jnp.int32), tok_rows, count).reshape(
        count_blocks, block
    )
    key_blocks = key_rows.reshape(count_blocks, block, heads, width)
    value_blocks = value_rows.reshape(count_blocks, block, heads, width)

    def advance(state, item):
        key_block, value_block, block_pos = item
        result = []
        for group in range(2):
            seen = jnp.min(block_pos) <= jnp.max(query_pos[group])
            result.append(
                lax.cond(
                    seen,
                    lambda inner, member=group: online_update(
                        inner,
                        groups[member],
                        query_pos[member],
                        key_block,
                        value_block,
                        block_pos,
                        scale,
                    ),
                    lambda inner: inner,
                    state[group],
                )
            )
        return (tuple(result), None)

    final_state, unused = lax.scan(advance, (blank, blank), (key_blocks, value_blocks, key_pos))
    outputs = [
        (summed / total[:, :, None]).astype(jnp.bfloat16) for leading, total, summed in final_state
    ]
    return jnp.concatenate(outputs, axis=0)


def attend_ranked(query_rows, query_ranks, keys, values, gate_rows):
    heads, rows, width = query_rows.shape
    block = math.gcd(rows, 512)
    scale = 1.0 / math.sqrt(width)
    key_ranks = jnp.arange(keys.shape[1], dtype=jnp.int32)

    def one_block(index):
        scores = (
            jnp.einsum("erd,ekd->erk", query_rows, keys, preferred_element_type=jnp.float32) * scale
        )
        visible = key_ranks[None, None, :] <= query_ranks[:, :, None]
        scores = jnp.where(visible, scores, NEGATIVE)
        leading = jnp.max(scores, axis=2, keepdims=True)
        weights = jnp.where(visible, jnp.exp(scores - leading), 0.0)
        total = jnp.sum(weights, axis=2, keepdims=True)
        mixed = (
            jnp.einsum(
                "erk,ekd->erd",
                weights.astype(jnp.bfloat16),
                values,
                preferred_element_type=jnp.float32,
            )
            / total
        )
        return (mixed * jax.nn.sigmoid(gate_rows.astype(jnp.float32))[:, :, None]).astype(
            jnp.bfloat16
        )

    blocks = lax.map(one_block, jnp.arange(rows // block, dtype=jnp.int32))
    return jnp.moveaxis(blocks, 0, 1).reshape(heads, rows, width)


def sparse_heads(queries, keys, values, gate_logit, selection):
    tok_rows, heads, width = queries.shape
    chosen = selection.shape[1]
    start = lax.axis_index("seq") * tok_rows
    positions = start + jnp.arange(tok_rows, dtype=jnp.int32)
    matches = selection[:, :, None] == positions[None, None, :]
    one_hot = matches.astype(jnp.bfloat16)

    def pick(source):
        return jnp.einsum(
            "ent,ted->end", one_hot, source, preferred_element_type=jnp.float32
        ).astype(jnp.bfloat16)

    gate_rows = jnp.einsum("ent,et->en", one_hot, gate_logit, preferred_element_type=jnp.float32)
    gathered = (
        lax.psum(pick(queries), "seq").astype(jnp.float32),
        lax.psum(pick(keys), "seq").astype(jnp.float32),
        lax.psum(pick(values), "seq").astype(jnp.float32),
        lax.psum(gate_rows.astype(jnp.bfloat16), "seq").astype(jnp.float32),
    )
    picked_q, picked_k, picked_v, picked_gate = [member.astype(jnp.bfloat16) for member in gathered]
    all_ranks = jnp.broadcast_to(jnp.arange(chosen, dtype=jnp.int32)[None, :], (heads, chosen))
    results = attend_ranked(picked_q, all_ranks, picked_k, picked_v, picked_gate)
    return jnp.einsum("ent,end->ted", one_hot, results, preferred_element_type=jnp.float32).astype(
        jnp.bfloat16
    )


def local(q_dense, k_dense, v_dense, q_expert, k_expert, v_expert, gate_logit, selection):
    dense_out = dense_heads(q_dense, k_dense, v_dense, plain_rows)
    expert_out = sparse_heads(q_expert, k_expert, v_expert, gate_logit, selection)
    return (dense_out, expert_out)


def solution(mesh):
    placed = (
        P(("dp", "seq"), "head", None),
        P(("dp", "seq"), "head", None),
        P(("dp", "seq"), "head", None),
        P(("dp", "seq"), "head", None),
        P(("dp", "seq"), "head", None),
        P(("dp", "seq"), "head", None),
        P("head", ("dp", "seq")),
        P("head", "dp"),
    )
    return jax.shard_map(
        local,
        mesh=mesh,
        in_specs=placed,
        out_specs=(P(("dp", "seq"), "head", None), P(("dp", "seq"), "head", None)),
        check_vma=False,
    )
```

profile of v0, /device:TPU:225, one launch (start us, length us, event | category | flops | bytes accessed | tf_op | source)
XLA Modules:
  0.0 332.1 jit_solution(16076033150022781153)
XLA Ops:
  8.2 2.1 fusion.67
  10.3 2.5 fusion.61
  12.7 1.4 fusion.64
  16.6 23.1 %psum.31 = bf16[3,512]{1,0:T(4,128)(2,1)S(1)} all-reduce(bf16[3,512]{1,0:T(4,128)(2,1)S(1)} %bitcast.68), channel_id=1, replica_groups=mesh['dp'=4,'head'=4,'seq'=16] {'seq'}, use_global_device_ids=true, to_apply=%region_18.19 | all-reduce | flops 1536 | bytes 6144 | tf_op jit(solution)/shard_map/psum | solution.py:133
  40.3 87.0 %all-reduce.3.cloned.1.call-done = (bf16[3,512,128]{2,1,0:T(8,128)(2,1)}, bf16[3,512,128]{2,1,0:T(8,128)(2,1)}, bf16[3,512,128]{2,1,0:T(8,128)(2,1)}) async-done(((bf16[3,512,128]{2,1,0:T(8,128)(2,1)}, bf16[3,512,128]{2,1,0:T(8,128)(2,1)}, bf16[3,512,128]{2,1,0:T(8,128)(2,1)}), (bf16[3,512,128]{2,1,0:T(8,128)(2,1)}, bf16[3,512,128]{2,1,0:T(8,128)(2,1)}, ...) | async-done | bytes 1179664 | tf_op jit(solution)/shard_map/psum | solution.py:132
  127.3 2.1 fusion.90
  129.5 1.6 fusion.73
  132.0 39.2 %all-gather.3.cloned.1.call-done = bf16[8192,2,128]{2,0,1:T(8,128)(2,1)} async-done(((bf16[512,2,128]{2,0,1:T(8,128)(2,1)}), bf16[8192,2,128]{2,0,1:T(8,128)(2,1)}) %all-gather.3.cloned.1.call-update) | async-done | bytes 4194320 | tf_op jit(solution)/shard_map/all_gather | solution.py:42
  171.2 42.6 %all-gather.5.cloned.1.call-done = bf16[8192,2,128]{2,0,1:T(8,128)(2,1)} async-done(((bf16[512,2,128]{2,0,1:T(8,128)(2,1)}), bf16[8192,2,128]{2,0,1:T(8,128)(2,1)}) %all-gather.5.cloned.1.call-update) | async-done | bytes 4194320 | tf_op jit(solution)/shard_map/all_gather | solution.py:43
  213.9 109.1 %while.26 = (s32[]{:T(128)}, f32[256,2]{0,1:T(2,128)S(1)}, f32[256,2]{0,1:T(2,128)S(1)}, f32[256,2,128]{2,0,1:T(8,128)S(1)}, f32[256,2]{0,1:T(2,128)S(1)}, /*ind...) while((s32[]{:T(128)}, f32[256,2]{0,1:T(2,128)S(1)}, ...), condition=%wide.region_12.13_spmd.clone, body=%wide.region_2.12_spmd.clone.sunk | while | flops 273682432 | bytes 10830257 | solution.py:76
  215.9 1.1 dynamic-slice_bitcast_fusion.3
  217.0 1.3 conditional.6
  219.4 1.3 conditional.7
  222.7 1.1 dynamic-slice_bitcast_fusion.3
  223.8 1.3 conditional.6
  226.3 1.3 conditional.7
  229.5 1.1 dynamic-slice_bitcast_fusion.3
  230.6 1.3 conditional.6
  233.1 1.3 conditional.7
  236.3 1.1 dynamic-slice_bitcast_fusion.3
  237.4 1.3 conditional.6
  239.9 1.3 conditional.7
  244.2 1.3 conditional.6
  246.7 1.3 conditional.7
  250.0 1.1 dynamic-slice_bitcast_fusion.3
  251.0 1.3 conditional.6
  253.5 1.3 conditional.7
  257.9 1.3 conditional.6
  260.3 1.3 conditional.7
  264.7 1.3 conditional.6
  267.2 1.3 conditional.7
  271.5 1.3 conditional.6
  274.0 1.3 conditional.7
  278.3 1.3 conditional.6
  280.8 1.3 conditional.7
  285.1 1.3 conditional.6
  287.6 1.3 conditional.7
  291.9 1.3 conditional.6
  294.4 1.3 conditional.7
  298.8 1.3 conditional.6
  301.2 1.3 conditional.7
  305.6 1.3 conditional.6
  308.1 1.3 conditional.7
  312.4 1.3 conditional.6
  314.9 1.3 conditional.7
  319.2 1.3 conditional.6
  321.7 1.3 conditional.7
  323.3 1.2 fusion.82
  (341 shorter events, 67.6 us)
Async XLA Ops:
  7.2 1.0 copy-start
  7.2 5.6 %copy-start.6 = (s32[3,512]{1,0:T(4,128)S(1)}, s32[3,512]{1,0:T(4,128)}, u32[]{:S(2)}) copy-start(s32[3,512]{1,0:T(4,128)} %param.21) | copy-start | bytes 18436
  7.2 5.5 %copy-start.4 = (bf16[512,3,128]{2,0,1:T(8,128)(2,1)S(1)}, bf16[512,3,128]{2,0,1:T(8,128)(2,1)}, u32[]{:S(2)}) copy-start(bf16[512,3,128]{2,0,1:T(8,128)(2,1)} %param.18) | copy-start | bytes 1179652
  7.2 120.1 %all-reduce.3.cloned.1.call-start = ((), (), s32[]{:S(2)}) async-start(), calls=%async_computation.2 | async-start | bytes 2359296 | tf_op jit(solution)/shard_map/psum | solution.py:132
  10.3 4.0 %copy-start.1 = (bf16[512,2,128]{2,1,0:T(2,128)(2,1)S(1)}, bf16[512,2,128]{2,1,0:T(2,128)(2,1)}, u32[]{:S(2)}) copy-start(bf16[512,2,128]{2,1,0:T(2,128)(2,1)} %param.15) | copy-start | bytes 786436
  10.3 4.8 %copy-start.2 = (bf16[512,2,128]{2,1,0:T(2,128)(2,1)S(1)}, bf16[512,2,128]{2,1,0:T(2,128)(2,1)}, u32[]{:S(2)}) copy-start(bf16[512,2,128]{2,1,0:T(2,128)(2,1)} %param.16) | copy-start | bytes 786436
  10.3 5.6 %copy-start.3 = (bf16[512,2,128]{2,1,0:T(2,128)(2,1)S(1)}, bf16[512,2,128]{2,1,0:T(2,128)(2,1)}, u32[]{:S(2)}) copy-start(bf16[512,2,128]{2,1,0:T(2,128)(2,1)} %param.14) | copy-start | bytes 786436
  12.7 3.2 copy-start.7
  14.2 157.1 %all-gather.3.cloned.1.call-start = ((), (), s32[]{:S(2)}) async-start(), calls=%async_computation | async-start | bytes 4456448 | tf_op jit(solution)/shard_map/all_gather | solution.py:42
  15.0 198.9 %all-gather.5.cloned.1.call-start = ((), (), s32[]{:S(2)}) async-start(), calls=%async_computation.1 | async-start | bytes 4456448 | tf_op jit(solution)/shard_map/all_gather | solution.py:43
  127.3 2.1 copy-start.5
Sparse Core Ops, SparseCore 0:
  14.3 113.0 all-reduce.2
  129.8 41.4 all-gather.2
  173.1 40.6 all-gather.4
where the time goes:
time: 333 us; the launch traced here: 332 us
  waiting for transfers between devices  169 us (51%)
  loops' own time  42.3 us (13%)
  matrix products  36.9 us (11%)
  other arithmetic  25.7 us (8%)
  blocking collectives  23.1 us (7%)
  local copies, waits for them, and re-layouts  21.1 us (6%)
  between operations  13.9 us (4%)
    psum x1, waiting for transfers between devices, sparse_heads(): lax.psum(pick(values), 'seq').astype(jnp.float32)  87 us
    all_gather x1, waiting for transfers between devices, dense_heads(): value_rows = lax.all_gather(values, 'seq', axis=0, tiled=True)  42.6 us
    another operation x1, loops' own time, dense_heads(): lax.scan(advance, (blank, blank), (key_blocks, value_blocks, key_pos))  40.4 us
    all_gather x1, waiting for transfers between devices, dense_heads(): key_rows = lax.all_gather(keys, 'seq', axis=0, tiled=True)  39.2 us
    psum x1, blocking collectives, sparse_heads(): lax.psum(gate_rows.astype(jnp.bfloat16), 'seq').astype(jnp.float32)  23.1 us
    squeeze x16, local copies, waits for them, and re-layouts, dense_heads(): lax.scan(advance, (blank, blank), (key_blocks, value_blocks, key_pos))  17.2 us
    dot_general x32, matrix products, online_update(): jnp.einsum('qhk,khd->qhd', weights.astype(jnp.bfloat16), values, preferre...  16.5 us
    reduce_min x16, other arithmetic, advance(): seen = jnp.min(block_pos) <= jnp.max(query_pos[group])  10.3 us
  transfers between devices with their start and end apart: 3, of which 3 were waited for; matrix products, arithmetic and copies ran while one was open for 2% of the time, Pallas kernels for 0%

commit v1 on v0

--- a/solution.py
+++ b/solution.py
@@ -5,6 +5,27 @@
 from jax.sharding import PartitionSpec as P
 
 NEGATIVE = -1e30
+
+
+def collect(shard, axis, dim):
+    size, index, rows = (lax.axis_size(axis), lax.axis_index(axis), shard.shape[dim])
+    forward = [(i, (i + 1) % size) for i in range(size)]
+    backward = [(i, (i - 1) % size) for i in range(size)]
+    result = jnp.zeros((*shard.shape[:dim], size * rows, *shard.shape[dim + 1 :]), shard.dtype)
+    result = lax.dynamic_update_slice_in_dim(result, shard, index * rows, axis=dim)
+    from_left = from_right = shard
+    half = size // 2
+    for turn in range(1, half + 1):
+        from_left = lax.ppermute(from_left, axis, forward)
+        result = lax.dynamic_update_slice_in_dim(
+            result, from_left, (index - turn) % size * rows, axis=dim
+        )
+        if turn < size - half:
+            from_right = lax.ppermute(from_right, axis, backward)
+            result = lax.dynamic_update_slice_in_dim(
+                result, from_right, (index + turn) % size * rows, axis=dim
+            )
+    return result
 
 
 def plain_rows(rows, tok_rows, count):
@@ -39,7 +60,7 @@
         jnp.zeros((half_rows, heads), jnp.float32),
         jnp.zeros((half_rows, heads, width), jnp.float32),
     )
-    key_rows = lax.all_gather(keys, "seq", axis=0, tiled=True)
+    key_rows = collect(keys, "seq", 0)
     value_rows = lax.all_gather(values, "seq", axis=0, tiled=True)
     length = key_rows.shape[0]
     block = math.gcd(length, 512)

time: 333 us -> 296 us (0.89)
  waiting for transfers between devices: 169 us -> 88.1 us
  starting transfers between devices: 0.12 us -> 25.1 us
  local copies, waits for them, and re-layouts: 21.1 us -> 34.4 us
    all_gather x1, waiting for transfers between devices: 42.6 us -> 0.57 us  [dense_heads(): value_rows = lax.all_gather(values, 'seq', axis=0, tiled=True)]
    all_gather x1 -> x0, waiting for transfers between devices: 39.2 us -> none  [dense_heads(): key_rows = lax.all_gather(keys, 'seq', axis=0, tiled=True)]
    ppermute x0 -> x15, starting transfers between devices: none -> 25 us  [the longest x8 24.3 us: collect(): from_left = lax.ppermute(from_left, axis, forward)]
    ppermute x0 -> x15, waiting for transfers between devices: none -> 21.4 us  [the longest x7 13.3 us: collect(): from_right = lax.ppermute(from_right, axis, backward)]
    psum x1, waiting for transfers between devices: 87 us -> 66.1 us  [sparse_heads(): lax.psum(pick(values), 'seq').astype(jnp.float32)]
    dynamic_update_slice x0 -> x15, local copies, waits for them, and re-layouts: none -> 10.8 us  [the longest x8 5.77 us: collect(): lax.dynamic_update_slice_in_dim(result, from_left, (index - turn) % size...]
  transfers between devices with their start and end apart: 3 -> 17, of which waited for: 3 -> 10; matrix products, arithmetic and copies ran while one was open for 2% -> 8% of each run, Pallas kernels for 0% -> 0%
where the time goes in v1:
time: 296 us; the launch traced here: 295 us
  waiting for transfers between devices  88.1 us (30%)
  loops' own time  44 us (15%)
  matrix products  39.7 us (13%)
  local copies, waits for them, and re-layouts  34.4 us (12%)
  other arithmetic  25.9 us (9%)
  starting transfers between devices  25.1 us (8%)
  blocking collectives  23.2 us (8%)
  between operations  14.3 us (5%)
    psum x1, waiting for transfers between devices, sparse_heads(): lax.psum(pick(values), 'seq').astype(jnp.float32)  66.1 us
    another operation x1, loops' own time, dense_heads(): lax.scan(advance, (blank, blank), (key_blocks, value_blocks, key_pos))  42.1 us
    ppermute x8, starting transfers between devices, collect(): from_left = lax.ppermute(from_left, axis, forward)  24.3 us
    psum x1, blocking collectives, sparse_heads(): lax.psum(gate_rows.astype(jnp.bfloat16), 'seq').astype(jnp.float32)  23.2 us
    squeeze x16, local copies, waits for them, and re-layouts, dense_heads(): lax.scan(advance, (blank, blank), (key_blocks, value_blocks, key_pos))  17.2 us
    dot_general x32, matrix products, online_update(): jnp.einsum('qhk,khd->qhd', weights.astype(jnp.bfloat16), values, preferre...  16.8 us
    ppermute x7, waiting for transfers between devices, collect(): from_right = lax.ppermute(from_right, axis, backward)  13.3 us
    reduce_min x16, other arithmetic, advance(): seen = jnp.min(block_pos) <= jnp.max(query_pos[group])  10.3 us
  transfers between devices with their start and end apart: 17, of which 10 were waited for; matrix products, arithmetic and copies ran while one was open for 8% of the time, Pallas kernels for 0%

profile of v1, /device:TPU:225, one launch (start us, length us, event | category | flops | bytes accessed | tf_op | source)
XLA Modules:
  0.0 294.7 jit_solution(14679742061539861037)
XLA Ops:
  8.2 2.1 fusion.67
  10.3 2.4 fusion.61
  12.7 1.4 fusion.64
  15.0 2.5 broadcast_in_dim.84
  19.6 23.2 %psum.31 = bf16[3,512]{1,0:T(4,128)(2,1)S(1)} all-reduce(bf16[3,512]{1,0:T(4,128)(2,1)S(1)} %bitcast.67), channel_id=1, replica_groups=mesh['dp'=4,'head'=4,'seq'=16] {'seq'}, use_global_device_ids=true, to_apply=%region_18.19 | all-reduce | flops 1536 | bytes 6144 | tf_op jit(solution)/shard_map/psum | solution.py:154
  42.9 3.5 %collective-permute-start.2 = (bf16[512,2,128]{2,0,1:T(8,128)(2,1)S(1)}, bf16[512,2,128]{2,0,1:T(8,128)(2,1)S(1)}, u32[]{:S(2)}, u32[]{:S(2)}) collective-permute-start(bf16[512,2,128]{2,0,1:T(8,128)(2,1)S(1)} %collective-permute-done), channel_id=1, source_target_pairs={{0,1},{1,2},{2,3},{3,4},{4,5},{5,6},{6,7},{7,8},{8,9},{9,10},{10,1... | collective-permute-start | bytes 786440 | tf_op jit(solution)/shard_map/ppermute | solution.py:19
  48.0 2.0 collective-permute-done.2
  50.0 3.8 %collective-permute-start.4 = (bf16[512,2,128]{2,0,1:T(8,128)(2,1)S(1)}, bf16[512,2,128]{2,0,1:T(8,128)(2,1)S(1)}, u32[]{:S(2)}, u32[]{:S(2)}) collective-permute-start(bf16[512,2,128]{2,0,1:T(8,128)(2,1)S(1)} %collective-permute-done.2), channel_id=1, source_target_pairs={{0,1},{1,2},{2,3},{3,4},{4,5},{5,6},{6,7},{7,8},{8,9},{9,10},{10,1... | collective-permute-start | bytes 786440 | tf_op jit(solution)/shard_map/ppermute | solution.py:19
  56.0 1.9 collective-permute-done.4
  57.9 3.7 %collective-permute-start.6 = (bf16[512,2,128]{2,0,1:T(8,128)(2,1)S(1)}, bf16[512,2,128]{2,0,1:T(8,128)(2,1)S(1)}, u32[]{:S(2)}, u32[]{:S(2)}) collective-permute-start(bf16[512,2,128]{2,0,1:T(8,128)(2,1)S(1)} %collective-permute-done.4), channel_id=1, source_target_pairs={{0,1},{1,2},{2,3},{3,4},{4,5},{5,6},{6,7},{7,8},{8,9},{9,10},{10,1... | collective-permute-start | bytes 786440 | tf_op jit(solution)/shard_map/ppermute | solution.py:19
  61.6 66.1 %all-reduce.3.cloned.1.call-done = (bf16[3,512,128]{2,1,0:T(8,128)(2,1)}, bf16[3,512,128]{2,1,0:T(8,128)(2,1)}, bf16[3,512,128]{2,1,0:T(8,128)(2,1)}) async-done(((bf16[3,512,128]{2,1,0:T(8,128)(2,1)}, bf16[3,512,128]{2,1,0:T(8,128)(2,1)}, bf16[3,512,128]{2,1,0:T(8,128)(2,1)}), (bf16[3,512,128]{2,1,0:T(8,128)(2,1)}, bf16[3,512,128]{2,1,0:T(8,128)(2,1)}, ...) | async-done | bytes 1179664 | tf_op jit(solution)/shard_map/psum | solution.py:153
  127.7 3.3 %fusion.91 = (f32[3,512]{1,0:T(4,128)S(1)}, bf16[3,512,512]{1,2,0:T(8,128)(2,1)}) fusion(bf16[3,512,128]{2,1,0:T(8,128)(2,1)} %get-tuple-element.319, bf16[3,512,128]{2,1,0:T(8,128)(2,1)} %get-tuple-element.320), kind=kOutput, calls=%fused_computation.114 | convolution fusion | flops 207618560 | bytes 2365440 | tf_op jit(solution)/shard_map/while/body/eval_jaxpr/sub | solution.py:117
  131.0 2.9 collective-permute-start.8
  134.0 3.0 %fusion.73 = bf16[512,3,128]{0,2,1:T(8,128)(2,1)S(1)} fusion(s32[512]{0:T(512)S(1)} %iota_add_fusion, s32[3,512]{1,0:T(4,128)S(1)} %copy-done.6, bf16[3,512,128]{2,1,0:T(8,128)(2,1)S(1)} %copy-done.5, bf16[3,512,512]{1,2,0:T(8,128)(2,1)} %get-tuple-element.336, f32[3,512]{1,0:T(4,128)S(1)} %add_divide_fusion, f32[3,512]{1,0:T(4,128)S(1)} %get-tuple-element.335), kind=kOutput, calls=%fused_computation.75 | convolution fusion | flops 404226048 | bytes 2379776 | tf_op jit(solution)/shard_map/ent,end->ted/dot_general | solution.py:159
  138.7 3.0 %collective-permute-start.10 = (bf16[512,2,128]{2,0,1:T(8,128)(2,1)S(1)}, bf16[512,2,128]{2,0,1:T(8,128)(2,1)S(1)}, u32[]{:S(2)}, u32[]{:S(2)}) collective-permute-start(bf16[512,2,128]{2,0,1:T(8,128)(2,1)S(1)} %collective-permute-done.8), channel_id=1, source_target_pairs={{0,1},{1,2},{2,3},{3,4},{4,5},{5,6},{6,7},{7,8},{8,9},{9,10},{10,1... | collective-permute-start | bytes 786440 | tf_op jit(solution)/shard_map/ppermute | solution.py:19
  143.1 4.4 %collective-permute-done.9 = bf16[512,2,128]{2,0,1:T(8,128)(2,1)S(1)} collective-permute-done((bf16[512,2,128]{2,0,1:T(8,128)(2,1)S(1)}, bf16[512,2,128]{2,0,1:T(8,128)(2,1)S(1)}, u32[]{:S(2)}, u32[]{:S(2)}) %collective-permute-start.9) | collective-permute-done | bytes 262176 | tf_op jit(solution)/shard_map/ppermute | solution.py:24
  148.3 2.1 collective-permute-done.10
  150.4 3.7 %collective-permute-start.12 = (bf16[512,2,128]{2,0,1:T(8,128)(2,1)S(1)}, bf16[512,2,128]{2,0,1:T(8,128)(2,1)S(1)}, u32[]{:S(2)}, u32[]{:S(2)}) collective-permute-start(bf16[512,2,128]{2,0,1:T(8,128)(2,1)S(1)} %collective-permute-done.10), channel_id=1, source_target_pairs={{0,1},{1,2},{2,3},{3,4},{4,5},{5,6},{6,7},{7,8},{8,9},{9,10},{10,1... | collective-permute-start | bytes 786440 | tf_op jit(solution)/shard_map/ppermute | solution.py:19
  155.5 4.4 %collective-permute-done.11 = bf16[512,2,128]{2,0,1:T(8,128)(2,1)S(1)} collective-permute-done((bf16[512,2,128]{2,0,1:T(8,128)(2,1)S(1)}, bf16[512,2,128]{2,0,1:T(8,128)(2,1)S(1)}, u32[]{:S(2)}, u32[]{:S(2)}) %collective-permute-start.11) | collective-permute-done | bytes 262176 | tf_op jit(solution)/shard_map/ppermute | solution.py:24
  160.6 2.0 collective-permute-done.12
  162.7 3.7 %collective-permute-start.14 = (bf16[512,2,128]{2,0,1:T(8,128)(2,1)S(1)}, bf16[512,2,128]{2,0,1:T(8,128)(2,1)S(1)}, u32[]{:S(2)}, u32[]{:S(2)}) collective-permute-start(bf16[512,2,128]{2,0,1:T(8,128)(2,1)S(1)} %collective-permute-done.12), channel_id=1, source_target_pairs={{0,1},{1,2},{2,3},{3,4},{4,5},{5,6},{6,7},{7,8},{8,9},{9,10},{10,1... | collective-permute-start | bytes 786440 | tf_op jit(solution)/shard_map/ppermute | solution.py:19
  167.8 4.4 %collective-permute-done.13 = bf16[512,2,128]{2,0,1:T(8,128)(2,1)S(1)} collective-permute-done((bf16[512,2,128]{2,0,1:T(8,128)(2,1)S(1)}, bf16[512,2,128]{2,0,1:T(8,128)(2,1)S(1)}, u32[]{:S(2)}, u32[]{:S(2)}) %collective-permute-start.13) | collective-permute-done | bytes 262176 | tf_op jit(solution)/shard_map/ppermute | solution.py:24
  174.3 111.0 %while.26 = (s32[]{:T(128)}, f32[256,2]{0,1:T(2,128)S(1)}, f32[256,2]{0,1:T(2,128)S(1)}, f32[256,2,128]{2,0,1:T(8,128)S(1)}, f32[256,2]{0,1:T(2,128)S(1)}, /*ind...) while((s32[]{:T(128)}, f32[256,2]{0,1:T(2,128)S(1)}, ...), condition=%wide.region_12.13_spmd.clone, body=%wide.region_2.12_spmd.clone.sunk | while | flops 273682432 | bytes 10830257 | solution.py:97
  177.4 1.3 conditional.6
  179.9 1.3 conditional.7
  184.3 1.3 conditional.6
  191.2 1.3 conditional.6
  193.8 1.3 conditional.7
  198.2 1.3 conditional.6
  200.7 1.3 conditional.7
  205.1 1.3 conditional.6
  212.1 1.3 conditional.6
  214.6 1.3 conditional.7
  219.0 1.3 conditional.6
  221.6 1.3 conditional.7
  225.9 1.3 conditional.6
  232.9 1.3 conditional.6
  235.4 1.3 conditional.7
  239.8 1.3 conditional.6
  242.4 1.3 conditional.7
  246.8 1.3 conditional.6
  253.7 1.3 conditional.6
  260.6 1.3 conditional.6
  263.2 1.3 conditional.7
  267.6 1.3 conditional.6
  274.5 1.3 conditional.6
  281.4 1.3 conditional.6
  284.0 1.3 conditional.7
  (384 shorter events, 95.8 us)
Async XLA Ops:
  7.2 1.0 copy-start
  7.2 5.5 %copy-start.6 = (s32[3,512]{1,0:T(4,128)S(1)}, s32[3,512]{1,0:T(4,128)}, u32[]{:S(2)}) copy-start(s32[3,512]{1,0:T(4,128)} %param.21) | copy-start | bytes 18436
  7.2 5.5 %copy-start.4 = (bf16[512,3,128]{2,0,1:T(8,128)(2,1)S(1)}, bf16[512,3,128]{2,0,1:T(8,128)(2,1)}, u32[]{:S(2)}) copy-start(bf16[512,3,128]{2,0,1:T(8,128)(2,1)} %param.18) | copy-start | bytes 1179652
  7.2 7.0 %copy-start.1 = (bf16[512,2,128]{2,1,0:T(2,128)(2,1)S(1)}, bf16[512,2,128]{2,1,0:T(2,128)(2,1)}, u32[]{:S(2)}) copy-start(bf16[512,2,128]{2,1,0:T(2,128)(2,1)} %param.16) | copy-start | bytes 786436
  7.2 120.4 %all-reduce.3.cloned.1.call-start = ((), (), s32[]{:S(2)}) async-start(), calls=%async_computation.1 | async-start | bytes 2359296 | tf_op jit(solution)/shard_map/psum | solution.py:153
  12.7 4.8 %copy-start.3 = (bf16[512,2,128]{2,1,0:T(2,128)(2,1)S(1)}, bf16[512,2,128]{2,1,0:T(2,128)(2,1)}, u32[]{:S(2)}) copy-start(bf16[512,2,128]{2,1,0:T(2,128)(2,1)} %param.15) | copy-start | bytes 786436
  12.7 6.3 %copy-start.7 = (bf16[3,512]{1,0:T(4,128)(2,1)S(1)}, bf16[3,512]{1,0:T(4,128)(2,1)}, u32[]{:S(2)}) copy-start(bf16[3,512]{1,0:T(4,128)(2,1)} %param.20) | copy-start | bytes 9220
  14.1 33.0 %copy-start.2 = (bf16[512,2,128]{2,1,0:T(2,128)(2,1)S(1)}, bf16[512,2,128]{2,1,0:T(2,128)(2,1)}, u32[]{:S(2)}) copy-start(bf16[512,2,128]{2,1,0:T(2,128)(2,1)} %param.14) | copy-start | bytes 786436
  14.2 160.0 %all-gather.2.cloned.1.call-start = ((), (), s32[]{:S(2)}) async-start(), calls=%async_computation | async-start | bytes 4456448 | tf_op jit(solution)/shard_map/all_gather | solution.py:64
  18.3 24.6 %collective-permute-start = (bf16[512,2,128]{2,0,1:T(8,128)(2,1)S(1)}, bf16[512,2,128]{2,0,1:T(8,128)(2,1)S(1)}, u32[]{:S(2)}, u32[]{:S(2)}) collective-permute-start(bf16[512,2,128]{2,0,1:T(8,128)(2,1)S(1)} %get-tuple-element.333), channel_id=1, source_target_pairs={{0,1},{1,2},{2,3},{3,4},{4,5},{5,6},{6,7},{7,8},{8,9},{9,10},{10,1... | collective-permute-start | bytes 786440 | tf_op jit(solution)/shard_map/ppermute | solution.py:19
  18.3 28.1 %collective-permute-start.1 = (bf16[512,2,128]{2,0,1:T(8,128)(2,1)S(1)}, bf16[512,2,128]{2,0,1:T(8,128)(2,1)S(1)}, u32[]{:S(2)}, u32[]{:S(2)}) collective-permute-start(bf16[512,2,128]{2,0,1:T(8,128)(2,1)S(1)} %get-tuple-element.333), channel_id=1, source_target_pairs={{0,15},{1,0},{2,1},{3,2},{4,3},{5,4},{6,5},{7,6},{8,7},{9,8},{10,9... | collective-permute-start | bytes 786440 | tf_op jit(solution)/shard_map/ppermute | solution.py:24
  42.9 7.1 %collective-permute-start.2 = (bf16[512,2,128]{2,0,1:T(8,128)(2,1)S(1)}, bf16[512,2,128]{2,0,1:T(8,128)(2,1)S(1)}, u32[]{:S(2)}, u32[]{:S(2)}) collective-permute-start(bf16[512,2,128]{2,0,1:T(8,128)(2,1)S(1)} %collective-permute-done), channel_id=1, source_target_pairs={{0,1},{1,2},{2,3},{3,4},{4,5},{5,6},{6,7},{7,8},{8,9},{9,10},{10,1... | collective-permute-start | bytes 786440 | tf_op jit(solution)/shard_map/ppermute | solution.py:19
  46.4 8.1 %collective-permute-start.3 = (bf16[512,2,128]{2,0,1:T(8,128)(2,1)S(1)}, bf16[512,2,128]{2,0,1:T(8,128)(2,1)S(1)}, u32[]{:S(2)}, u32[]{:S(2)}) collective-permute-start(bf16[512,2,128]{2,0,1:T(8,128)(2,1)S(1)} %collective-permute-done.1), channel_id=1, source_target_pairs={{0,15},{1,0},{2,1},{3,2},{4,3},{5,4},{6,5},{7,6},{8,7},{9,8},{10,9... | collective-permute-start | bytes 786440 | tf_op jit(solution)/shard_map/ppermute | solution.py:24
  50.0 7.9 %collective-permute-start.4 = (bf16[512,2,128]{2,0,1:T(8,128)(2,1)S(1)}, bf16[512,2,128]{2,0,1:T(8,128)(2,1)S(1)}, u32[]{:S(2)}, u32[]{:S(2)}) collective-permute-start(bf16[512,2,128]{2,0,1:T(8,128)(2,1)S(1)} %collective-permute-done.2), channel_id=1, source_target_pairs={{0,1},{1,2},{2,3},{3,4},{4,5},{5,6},{6,7},{7,8},{8,9},{9,10},{10,1... | collective-permute-start | bytes 786440 | tf_op jit(solution)/shard_map/ppermute | solution.py:19
  54.5 76.5 %collective-permute-start.5 = (bf16[512,2,128]{2,0,1:T(8,128)(2,1)S(1)}, bf16[512,2,128]{2,0,1:T(8,128)(2,1)S(1)}, u32[]{:S(2)}, u32[]{:S(2)}) collective-permute-start(bf16[512,2,128]{2,0,1:T(8,128)(2,1)S(1)} %collective-permute-done.3), channel_id=1, source_target_pairs={{0,15},{1,0},{2,1},{3,2},{4,3},{5,4},{6,5},{7,6},{8,7},{9,8},{10,9... | collective-permute-start | bytes 786440 | tf_op jit(solution)/shard_map/ppermute | solution.py:24
  57.9 73.1 %collective-permute-start.6 = (bf16[512,2,128]{2,0,1:T(8,128)(2,1)S(1)}, bf16[512,2,128]{2,0,1:T(8,128)(2,1)S(1)}, u32[]{:S(2)}, u32[]{:S(2)}) collective-permute-start(bf16[512,2,128]{2,0,1:T(8,128)(2,1)S(1)} %collective-permute-done.4), channel_id=1, source_target_pairs={{0,1},{1,2},{2,3},{3,4},{4,5},{5,6},{6,7},{7,8},{8,9},{9,10},{10,1... | collective-permute-start | bytes 786440 | tf_op jit(solution)/shard_map/ppermute | solution.py:19
  127.7 6.3 %copy-start.5 = (bf16[3,512,128]{2,1,0:T(8,128)(2,1)S(1)}, bf16[3,512,128]{2,1,0:T(8,128)(2,1)}, u32[]{:S(2)}) copy-start(bf16[3,512,128]{2,1,0:T(8,128)(2,1)} %get-tuple-element.318) | copy-start | bytes 1179652
  131.0 7.0 %collective-permute-start.7 = (bf16[512,2,128]{2,0,1:T(8,128)(2,1)S(1)}, bf16[512,2,128]{2,0,1:T(8,128)(2,1)S(1)}, u32[]{:S(2)}, u32[]{:S(2)}) collective-permute-start(bf16[512,2,128]{2,0,1:T(8,128)(2,1)S(1)} %collective-permute-done.5), channel_id=1, source_target_pairs={{0,15},{1,0},{2,1},{3,2},{4,3},{5,4},{6,5},{7,6},{8,7},{9,8},{10,9... | collective-permute-start | bytes 786440 | tf_op jit(solution)/shard_map/ppermute | solution.py:24
  131.0 7.7 %collective-permute-start.8 = (bf16[512,2,128]{2,0,1:T(8,128)(2,1)S(1)}, bf16[512,2,128]{2,0,1:T(8,128)(2,1)S(1)}, u32[]{:S(2)}, u32[]{:S(2)}) collective-permute-start(bf16[512,2,128]{2,0,1:T(8,128)(2,1)S(1)} %collective-permute-done.6), channel_id=1, source_target_pairs={{0,1},{1,2},{2,3},{3,4},{4,5},{5,6},{6,7},{7,8},{8,9},{9,10},{10,1... | collective-permute-start | bytes 786440 | tf_op jit(solution)/shard_map/ppermute | solution.py:19
  138.0 9.6 %collective-permute-start.9 = (bf16[512,2,128]{2,0,1:T(8,128)(2,1)S(1)}, bf16[512,2,128]{2,0,1:T(8,128)(2,1)S(1)}, u32[]{:S(2)}, u32[]{:S(2)}) collective-permute-start(bf16[512,2,128]{2,0,1:T(8,128)(2,1)S(1)} %collective-permute-done.7), channel_id=1, source_target_pairs={{0,15},{1,0},{2,1},{3,2},{4,3},{5,4},{6,5},{7,6},{8,7},{9,8},{10,9... | collective-permute-start | bytes 786440 | tf_op jit(solution)/shard_map/ppermute | solution.py:24
  138.7 11.7 %collective-permute-start.10 = (bf16[512,2,128]{2,0,1:T(8,128)(2,1)S(1)}, bf16[512,2,128]{2,0,1:T(8,128)(2,1)S(1)}, u32[]{:S(2)}, u32[]{:S(2)}) collective-permute-start(bf16[512,2,128]{2,0,1:T(8,128)(2,1)S(1)} %collective-permute-done.8), channel_id=1, source_target_pairs={{0,1},{1,2},{2,3},{3,4},{4,5},{5,6},{6,7},{7,8},{8,9},{9,10},{10,1... | collective-permute-start | bytes 786440 | tf_op jit(solution)/shard_map/ppermute | solution.py:19
  147.6 12.3 %collective-permute-start.11 = (bf16[512,2,128]{2,0,1:T(8,128)(2,1)S(1)}, bf16[512,2,128]{2,0,1:T(8,128)(2,1)S(1)}, u32[]{:S(2)}, u32[]{:S(2)}) collective-permute-start(bf16[512,2,128]{2,0,1:T(8,128)(2,1)S(1)} %collective-permute-done.9), channel_id=1, source_target_pairs={{0,15},{1,0},{2,1},{3,2},{4,3},{5,4},{6,5},{7,6},{8,7},{9,8},{10,9... | collective-permute-start | bytes 786440 | tf_op jit(solution)/shard_map/ppermute | solution.py:24
  150.4 12.3 %collective-permute-start.12 = (bf16[512,2,128]{2,0,1:T(8,128)(2,1)S(1)}, bf16[512,2,128]{2,0,1:T(8,128)(2,1)S(1)}, u32[]{:S(2)}, u32[]{:S(2)}) collective-permute-start(bf16[512,2,128]{2,0,1:T(8,128)(2,1)S(1)} %collective-permute-done.10), channel_id=1, source_target_pairs={{0,1},{1,2},{2,3},{3,4},{4,5},{5,6},{6,7},{7,8},{8,9},{9,10},{10,1... | collective-permute-start | bytes 786440 | tf_op jit(solution)/shard_map/ppermute | solution.py:19
  159.9 12.3 %collective-permute-start.13 = (bf16[512,2,128]{2,0,1:T(8,128)(2,1)S(1)}, bf16[512,2,128]{2,0,1:T(8,128)(2,1)S(1)}, u32[]{:S(2)}, u32[]{:S(2)}) collective-permute-start(bf16[512,2,128]{2,0,1:T(8,128)(2,1)S(1)} %collective-permute-done.11), channel_id=1, source_target_pairs={{0,15},{1,0},{2,1},{3,2},{4,3},{5,4},{6,5},{7,6},{8,7},{9,8},{10,9... | collective-permute-start | bytes 786440 | tf_op jit(solution)/shard_map/ppermute | solution.py:24
  162.7 10.2 %collective-permute-start.14 = (bf16[512,2,128]{2,0,1:T(8,128)(2,1)S(1)}, bf16[512,2,128]{2,0,1:T(8,128)(2,1)S(1)}, u32[]{:S(2)}, u32[]{:S(2)}) collective-permute-start(bf16[512,2,128]{2,0,1:T(8,128)(2,1)S(1)} %collective-permute-done.12), channel_id=1, source_target_pairs={{0,1},{1,2},{2,3},{3,4},{4,5},{5,6},{6,7},{7,8},{8,9},{9,10},{10,1... | collective-permute-start | bytes 786440 | tf_op jit(solution)/shard_map/ppermute | solution.py:19
Sparse Core Ops, SparseCore 0:
  14.3 113.3 all-reduce.2
  130.1 44.0 all-gather.1
